TPU v7x, 128 devices: a whole 4x4x4 slice. The times are simulated.
128 devices in a mesh: row: 8 (over z, core), col: 16 (over y, x).
Axes of the slice: x: 4, y: 4, z: 4, core: 2. Of those that a mesh axis runs over, the one named last changes fastest.
Arguments:
- psi_val: float32 [64, 128, 128, 128], P(None, 'row', 'col'), may hold values from -6 to 6
- psi_cond: float32 [64, 128, 128, 128], P(None, 'row', 'col'), may hold values from -6 to 6
- eps_val: float32 [64], replicated, may hold values from -12 to -1
- eps_cond: float32 [64], replicated, may hold values from 1 to 12
- val_index: int32 [128], replicated, may hold values from 0 to 63
- cond_index: int32 [128], replicated, may hold values from 0 to 63
- gmap: int32 [8192], replicated, may hold values from 0 to 2097151, as said below
- chi0_in: float32 [2, 8192, 8192], P(None, 'row', 'col'), may hold values from -6 to 6
Outputs:
- chi0_out: float32 [2, 8192, 8192], P(None, 'row', 'col')
Inputs may be any that keep to these rules, and one draw needn't show every extreme that they name: gmap holds 8192 distinct entries. Entries g of device block d = g // 64 (d = r * 16 + c) have ky in [r * 16, (r + 1) * 16) and kz in [c * 8, (c + 1) * 8); kx is any.
All inputs are finite; a program needn't handle non-finite values.
Results may differ from a plain program's by a relative error of at most 0.000068.
Values sent between devices are 32-bit elements; how exact they have to be, the bound alone decides.
No kernel may reach another device: no remote copies, remote signals or barrier semaphores. Data moves between devices by JAX's collectives and lax.ppermute only.
A program may use at most 128 MiB of HBM per device.

v0:
```python
import math

import jax
import jax.numpy as jnp
from jax import lax
from jax.sharding import PartitionSpec as P

GRID = 128
NG = 8192


HIGH = lax.Precision.HIGHEST


def spread(block, axis, holder):
    block = jnp.where(lax.axis_index(axis) == holder, block, jnp.zeros_like(block))
    return lax.psum(block, axis)


def dft_tables(length):
    steps = jnp.arange(length, dtype=jnp.int32)
    phase = steps[:, None] * steps[None, :] % length
    angle = phase.astype(jnp.float32) * (2.0 * math.pi / length)
    return (jnp.cos(angle), jnp.sin(angle))


def point_tables(freq_x, length):
    steps = jnp.arange(length, dtype=jnp.int32)
    phase = steps[:, None] * freq_x[None, :] % length
    angle = phase.astype(jnp.float32) * (2.0 * math.pi / length)
    return (jnp.cos(angle), jnp.sin(angle))


def pick_points(real_part, imag_part, yz_index, cos_x, sin_x):
    count = real_part.shape[0]
    flat_re = real_part.reshape(count, real_part.shape[1], -1)
    flat_im = imag_part.reshape(count, imag_part.shape[1], -1)
    cols_re = jnp.take(flat_re, yz_index, axis=2)
    cols_im = jnp.take(flat_im, yz_index, axis=2)
    m_re = jnp.sum(cols_re * cos_x[None] + cols_im * sin_x[None], axis=1)
    m_im = jnp.sum(cols_im * cos_x[None] - cols_re * sin_x[None], axis=1)
    return (m_re, m_im)


def contract_pairs(left, right):
    return lax.dot_general(
        left, right, (((0,), (0,)), ((), ())), precision=HIGH, preferred_element_type=jnp.float32
    )


def on_device(psi_val, psi_cond, eps_val, eps_cond, val_index, cond_index, gmap, chi0_in):
    pairs = val_index.shape[0]
    scale = 1.0 / math.sqrt(GRID**3)
    cos_t, sin_t = dft_tables(GRID)
    rho = jnp.take(psi_val, val_index, axis=0) * jnp.take(psi_cond, cond_index, axis=0)
    row_pos = lax.axis_index("row")
    col_pos = lax.axis_index("col")
    mesh_cols = lax.axis_size("col")
    mesh_rows = lax.axis_size("row")
    per_device = NG // (mesh_rows * mesh_cols)
    row_span = GRID // mesh_rows
    col_span = GRID // mesh_cols
    flat_pos = row_pos * mesh_cols + col_pos
    own_map = lax.dynamic_slice_in_dim(gmap, flat_pos * per_device, per_device, 0)
    freq_x = own_map // (GRID * GRID)
    freq_y = own_map // GRID % GRID - row_pos * row_span
    freq_z = own_map % GRID - col_pos * col_span
    yz_index = freq_y * col_span + freq_z
    cos_x, sin_x = point_tables(freq_x, GRID)
    z_re = jnp.einsum("pxyz,zk->pxyk", rho, cos_t, precision=HIGH)
    z_im = -jnp.einsum("pxyz,zk->pxyk", rho, sin_t, precision=HIGH)
    part_re = lax.all_to_all(z_re, "col", split_axis=3, concat_axis=2, tiled=True)
    part_im = lax.all_to_all(z_im, "col", split_axis=3, concat_axis=2, tiled=True)
    y_re = jnp.einsum("pxyz,yk->pxkz", part_re, cos_t, precision=HIGH) + jnp.einsum(
        "pxyz,yk->pxkz", part_im, sin_t, precision=HIGH
    )
    y_im = jnp.einsum("pxyz,yk->pxkz", part_im, cos_t, precision=HIGH) - jnp.einsum(
        "pxyz,yk->pxkz", part_re, sin_t, precision=HIGH
    )
    y_re, y_im = (y_re, y_im)
    m_re, m_im = pick_points(
        lax.all_to_all(y_re, "row", split_axis=2, concat_axis=1, tiled=True),
        lax.all_to_all(y_im, "row", split_axis=2, concat_axis=1, tiled=True),
        yz_index,
        cos_x,
        sin_x,
    )
    m_re = m_re * scale
    m_im = m_im * scale
    cols_span = chi0_in.shape[2]
    rows_re, rows_im = (
        lax.all_gather(m_re, "col", axis=1, tiled=True),
        lax.all_gather(m_im, "col", axis=1, tiled=True),
    )
    offset = col_pos * mesh_rows % mesh_cols * per_device
    piece_re = lax.dynamic_slice_in_dim(rows_re, offset, cols_span, 1)
    piece_im = lax.dynamic_slice_in_dim(rows_im, offset, cols_span, 1)
    root = col_pos * mesh_rows // mesh_cols
    cols_re, cols_im = (spread(piece_re, "row", root), spread(piece_im, "row", root))
    val_hot = val_index[:, None] == jnp.arange(eps_val.shape[0], dtype=jnp.int32)[None, :]
    cond_hot = cond_index[:, None] == jnp.arange(eps_cond.shape[0], dtype=jnp.int32)[None, :]
    energy_v = jnp.sum(jnp.where(val_hot, eps_val[None, :], 0.0), axis=1)
    energy_c = jnp.sum(jnp.where(cond_hot, eps_cond[None, :], 0.0), axis=1)
    weight = (-6.0 / (math.sqrt(pairs) * (energy_c - energy_v)))[:, None]
    out_re = (
        chi0_in[0]
        + contract_pairs(weight * rows_re, cols_re)
        + contract_pairs(weight * rows_im, cols_im)
    )
    out_im = (
        chi0_in[1]
        + contract_pairs(weight * rows_im, cols_re)
        - contract_pairs(weight * rows_re, cols_im)
    )
    return jnp.stack([out_re, out_im])


def solution(mesh):
    return jax.shard_map(
        on_device,
        mesh=mesh,
        in_specs=(
            P(None, "row", "col", None),
            P(None, "row", "col", None),
            P(),
            P(),
            P(),
            P(),
            P(),
            P(None, "row", "col"),
        ),
        out_specs=P(None, "row", "col"),
        check_vma=False,
    )
```

profile of v0, /device:TPU:24, one launch (start us, length us, event | category | flops | bytes accessed | tf_op | source)
XLA Modules:
  0.0 715.7 jit_solution(10853611819511883215)
XLA Ops:
  6.5 0.7 compare_select_fusion.1
  7.2 0.7 compare_and_fusion.1
  7.9 6.5 gather_fusion.1
  14.4 6.5 gather_fusion
  20.9 6.5 select_multiply_fusion
  27.4 3.2 copy-done
  30.7 14.7 %fusion.6 = f32[128,16,8,128]{3,0,2,1:T(8,128)} fusion(f32[128,16,8,128]{3,2,1,0:T(8,128)S(1)} %select_multiply_fusion), kind=kOutput, calls=%fused_computation.18 | convolution fusion | flops 3223552000 | bytes 16777216 | tf_op jit(solution)/shard_map/pxyz,zk->pxyk/dot_general | solution.py:71
  45.4 9.3 %copy.79 = f32[128,16,8,128]{0,2,1,3:T(8,128)} copy(f32[128,16,8,128]{3,0,2,1:T(8,128)} %fusion.6) | data formatting | bytes 16777216 | tf_op jit(solution)/shard_map/neg | solution.py:71
  54.7 7.5 %all-to-all-start.1 = ((f32[128,16,8,128]{0,2,1,3:T(8,128)}), f32[128,16,8,128]{0,2,1,3:T(8,128)}, u32[]{:S(2)}, u32[]{:S(2)}) async-start(f32[128,16,8,128]{0,2,1,3:T(8,128)} %copy.79), calls=%async_computation.1 | async-start | bytes 16777216 | tf_op jit(solution)/shard_map/all_to_all | solution.py:73
  62.2 11.3 %fusion.29 = f32[128,16,8,128]{3,2,1,0:T(8,128)} fusion(f32[128,16,8,128]{3,2,1,0:T(8,128)} %copy-done), kind=kOutput, calls=%fused_computation.46 | convolution fusion | flops 3221454848 | bytes 16777216 | tf_op jit(solution)/shard_map/pxyz,zk->pxyk/dot_general | solution.py:70
  73.5 9.3 %copy.73 = f32[128,16,8,128]{0,2,1,3:T(8,128)} copy(f32[128,16,8,128]{3,2,1,0:T(8,128)} %fusion.29) | data formatting | bytes 16777216 | tf_op jit(solution)/shard_map/pxyz,zk->pxyk/dot_general | solution.py:70
  82.8 102.7 %all-to-all-done.1 = f32[128,16,8,128]{0,2,1,3:T(8,128)} async-done(((f32[128,16,8,128]{0,2,1,3:T(8,128)}), f32[128,16,8,128]{0,2,1,3:T(8,128)}, u32[]{:S(2)}, u32[]{:S(2)}) %all-to-all-start.1) | async-done | bytes 8388640 | tf_op jit(solution)/shard_map/all_to_all | solution.py:73
  185.5 6.4 all-to-all-start
  191.9 11.5 %copy.81 = f32[128,16,16,8,8]{0,4,3,2,1:T(8,128)} copy(f32[128,16,16,8,8]{0,3,1,4,2:T(8,128)} %bitcast.13) | data formatting | bytes 16777216 | tf_op jit(solution)/shard_map/all_to_all | solution.py:73
  203.3 9.3 %copy.82 = f32[128,16,128,8]{2,0,3,1:T(8,128)} copy(f32[128,16,128,8]{0,3,2,1:T(8,128)} %bitcast.83) | data formatting | bytes 16777216 | tf_op jit(solution)/shard_map/all_to_all | solution.py:73
  212.6 12.3 %fusion.31 = f32[128,128,16,8]{1,0,3,2:T(8,128)} fusion(f32[128,16,128,8]{2,0,3,1:T(8,128)} %copy.82), kind=kOutput, calls=%fused_computation.48 | convolution fusion | flops 3221454848 | bytes 16777216 | tf_op jit(solution)/shard_map/pxyz,yk->pxkz/dot_general | solution.py:77
  224.9 88.0 %all-to-all-done = f32[128,16,8,128]{0,2,1,3:T(8,128)} async-done(((f32[128,16,8,128]{0,2,1,3:T(8,128)}), f32[128,16,8,128]{0,2,1,3:T(8,128)}, u32[]{:S(2)}, u32[]{:S(2)}) %all-to-all-start) | async-done | bytes 8388640 | tf_op jit(solution)/shard_map/all_to_all | solution.py:72
  312.9 11.5 %copy.75 = f32[128,16,16,8,8]{0,4,3,2,1:T(8,128)} copy(f32[128,16,16,8,8]{0,3,1,4,2:T(8,128)} %bitcast.6) | data formatting | bytes 16777216 | tf_op jit(solution)/shard_map/all_to_all | solution.py:72
  324.4 9.3 %copy.76 = f32[128,16,128,8]{2,0,3,1:T(8,128)} copy(f32[128,16,128,8]{0,3,2,1:T(8,128)} %bitcast.84) | data formatting | bytes 16777216 | tf_op jit(solution)/shard_map/all_to_all | solution.py:72
  333.7 12.4 %subtract_bitcast_fusion = f32[128,16,128,8]{0,2,3,1:T(8,128)S(1)} fusion(f32[128,128,16,8]{1,0,3,2:T(8,128)} %fusion.31, f32[128,16,128,8]{2,0,3,1:T(8,128)} %copy.76), kind=kOutput, calls=%fused_computation.7 | convolution fusion | flops 3223552000 | bytes 25165824 | tf_op jit(solution)/shard_map/pxyz,yk->pxkz/dot_general | solution.py:77
  346.1 8.1 %copy.89 = f32[128,16,128,8]{0,3,1,2:T(8,128)} copy(f32[128,16,128,8]{0,2,3,1:T(8,128)S(1)} %subtract_bitcast_fusion) | data formatting | bytes 16777216 | tf_op jit(solution)/shard_map/sub | solution.py:77
  354.2 5.6 all-to-all-start.3
  359.8 10.0 %fusion.33 = f32[128,128,16,8]{1,0,3,2:T(8,128)S(1)} fusion(f32[128,16,128,8]{2,0,3,1:T(8,128)} %copy.76), kind=kOutput, calls=%fused_computation.50 | convolution fusion | flops 3221454848 | bytes 16777216 | tf_op jit(solution)/shard_map/pxyz,yk->pxkz/dot_general | solution.py:74
  369.8 10.3 %add_bitcast_fusion = f32[128,16,128,8]{0,2,3,1:T(8,128)S(1)} fusion(f32[128,128,16,8]{1,0,3,2:T(8,128)S(1)} %fusion.33, f32[128,16,128,8]{2,0,3,1:T(8,128)} %copy.82), kind=kOutput, calls=%fused_computation.8 | convolution fusion | flops 3223552000 | bytes 25165824 | tf_op jit(solution)/shard_map/pxyz,yk->pxkz/dot_general | solution.py:74
  380.1 8.1 %copy.83 = f32[128,16,128,8]{0,3,1,2:T(8,128)} copy(f32[128,16,128,8]{0,2,3,1:T(8,128)S(1)} %add_bitcast_fusion) | data formatting | bytes 16777216 | tf_op jit(solution)/shard_map/add | solution.py:74
  388.2 66.2 %all-to-all-done.3 = f32[128,16,128,8]{0,3,1,2:T(8,128)} async-done(((f32[128,16,128,8]{0,3,1,2:T(8,128)}), f32[128,16,128,8]{0,3,1,2:T(8,128)}, u32[]{:S(2)}, u32[]{:S(2)}) %all-to-all-start.3) | async-done | bytes 8388640 | tf_op jit(solution)/shard_map/all_to_all | solution.py:83
  454.4 4.9 all-to-all-start.2
  459.4 0.8 and_select_fusion
  460.2 0.8 compare_and_fusion
  461.0 0.2 fusion.53
  461.2 7.8 %copy.91 = f32[128,8,16,16,8]{0,4,3,2,1:T(8,128)} copy(f32[128,8,16,16,8]{0,4,2,3,1:T(8,128)} %bitcast.26) | data formatting | bytes 16777216 | tf_op jit(solution)/shard_map/all_to_all | solution.py:83
  469.0 9.3 %copy.92 = f32[128,128,128]{1,0,2:T(8,128)} copy(f32[128,128,128]{0,2,1:T(8,128)} %bitcast.85) | data formatting | bytes 16777216 | tf_op jit(solution)/shard_map/reshape | solution.py:37
  478.3 75.7 %all-to-all-done.2 = f32[128,16,128,8]{0,3,1,2:T(8,128)} async-done(((f32[128,16,128,8]{0,3,1,2:T(8,128)}), f32[128,16,128,8]{0,3,1,2:T(8,128)}, u32[]{:S(2)}, u32[]{:S(2)}) %all-to-all-start.2) | async-done | bytes 8388640 | tf_op jit(solution)/shard_map/all_to_all | solution.py:82
  554.0 7.8 %copy.85 = f32[128,8,16,16,8]{0,4,3,2,1:T(8,128)} copy(f32[128,8,16,16,8]{0,4,2,3,1:T(8,128)} %bitcast.18) | data formatting | bytes 16777216 | tf_op jit(solution)/shard_map/all_to_all | solution.py:82
  561.7 9.3 %copy.86 = f32[128,128,128]{1,0,2:T(8,128)} copy(f32[128,128,128]{0,2,1:T(8,128)} %bitcast.86) | data formatting | bytes 16777216 | tf_op jit(solution)/shard_map/reshape | solution.py:36
  571.1 6.2 gather_fusion.3
  577.3 6.2 gather_fusion.2
  583.5 4.9 fusion.5
  588.4 22.0 %all_gather.6 = f32[128,1024]{0,1:T(8,128)S(1)} all-gather(f32[128,64]{0,1:T(8,128)S(1)} %broadcast_multiply_fusion.1), channel_id=1, replica_groups=mesh['row'=8,'col'=16] {'col'}, dimensions={1}, use_global_device_ids=true | all-gather | bytes 557056 | tf_op jit(solution)/shard_map/all_gather | solution.py:92
  610.4 23.4 %all_gather.7 = f32[128,1024]{0,1:T(8,128)S(1)} all-gather(f32[128,64]{0,1:T(8,128)S(1)} %broadcast_multiply_fusion), channel_id=1, replica_groups=mesh['row'=8,'col'=16] {'col'}, dimensions={1}, use_global_device_ids=true | all-gather | bytes 557056 | tf_op jit(solution)/shard_map/all_gather | solution.py:93
  633.8 0.7 dynamic-slice_select_fusion.1
  634.6 0.7 dynamic-slice_select_fusion
  635.5 59.1 %all-reduce.3.cloned.1.call-done = (f32[128,512]{0,1:T(8,128)}, f32[128,512]{0,1:T(8,128)}) async-done(((f32[128,512]{0,1:T(8,128)}, f32[128,512]{0,1:T(8,128)}), (f32[128,512]{0,1:T(8,128)}, f32[128,512]{0,1:T(8,128)})) %all-reduce.3.cloned.1.call-update) | async-done | bytes 524304 | tf_op jit(solution)/shard_map/psum | solution.py:17
  694.6 2.9 fusion.13
  697.5 2.7 fusion.17
  700.2 3.7 fusion.10
  703.9 2.0 fusion.12
  705.9 2.5 pad_maximum_fusion
  (22 shorter events, 0.2 us)
Async XLA Ops:
  27.4 3.2 copy-start
  54.7 130.8 %all-to-all-start.1 = ((f32[128,16,8,128]{0,2,1,3:T(8,128)}), f32[128,16,8,128]{0,2,1,3:T(8,128)}, u32[]{:S(2)}, u32[]{:S(2)}) async-start(f32[128,16,8,128]{0,2,1,3:T(8,128)} %copy.79), calls=%async_computation.1 | async-start | bytes 16777216 | tf_op jit(solution)/shard_map/all_to_all | solution.py:73
  185.5 127.4 %all-to-all-start = ((f32[128,16,8,128]{0,2,1,3:T(8,128)}), f32[128,16,8,128]{0,2,1,3:T(8,128)}, u32[]{:S(2)}, u32[]{:S(2)}) async-start(f32[128,16,8,128]{0,2,1,3:T(8,128)} %copy.73), calls=%async_computation | async-start | bytes 16777216 | tf_op jit(solution)/shard_map/all_to_all | solution.py:72
  354.2 100.2 %all-to-all-start.3 = ((f32[128,16,128,8]{0,3,1,2:T(8,128)}), f32[128,16,128,8]{0,3,1,2:T(8,128)}, u32[]{:S(2)}, u32[]{:S(2)}) async-start(f32[128,16,128,8]{0,3,1,2:T(8,128)} %copy.89), calls=%async_computation.3 | async-start | bytes 16777216 | tf_op jit(solution)/shard_map/all_to_all | solution.py:83
  454.4 99.6 %all-to-all-start.2 = ((f32[128,16,128,8]{0,3,1,2:T(8,128)}), f32[128,16,128,8]{0,3,1,2:T(8,128)}, u32[]{:S(2)}, u32[]{:S(2)}) async-start(f32[128,16,128,8]{0,3,1,2:T(8,128)} %copy.83), calls=%async_computation.2 | async-start | bytes 16777216 | tf_op jit(solution)/shard_map/all_to_all | solution.py:82
  459.4 235.2 %all-reduce.3.cloned.1.call-start = ((), (), s32[]{:S(2)}) async-start(), calls=%async_computation.4 | async-start | bytes 1048576 | tf_op jit(solution)/shard_map/psum | solution.py:17
  583.4 51.9 %copy-start.3 = (s32[128]{0:T(128)S(1)}, s32[128]{0:T(128)}, u32[]{:S(2)}) copy-start(s32[128]{0:T(128)} %param.17) | copy-start | bytes 1540
  583.4 51.9 %copy-start.4 = (s32[128]{0:T(128)S(1)}, s32[128]{0:T(128)}, u32[]{:S(2)}) copy-start(s32[128]{0:T(128)} %param.16) | copy-start | bytes 1540
  583.4 51.9 %copy-start.5 = (f32[64]{0:T(128)S(1)}, f32[64]{0:T(128)}, u32[]{:S(2)}) copy-start(f32[64]{0:T(128)} %param.14) | copy-start | bytes 772
  583.5 51.9 %copy-start.6 = (f32[64]{0:T(128)S(1)}, f32[64]{0:T(128)}, u32[]{:S(2)}) copy-start(f32[64]{0:T(128)} %param.15) | copy-start | bytes 772
  694.5 9.3 %copy-start.1 = (f32[2,1024,512]{2,1,0:T(8,128)S(1)}, f32[2,1024,512]{2,1,0:T(8,128)}, u32[]{:S(2)}) copy-start(f32[2,1024,512]{2,1,0:T(8,128)} %param.19) | copy-start | bytes 12582916
  694.6 9.4 %copy-start.2 = (f32[128,512]{0,1:T(8,128)S(1)}, f32[128,512]{0,1:T(8,128)}, u32[]{:S(2)}) copy-start(f32[128,512]{0,1:T(8,128)} %get-tuple-element.10) | copy-start | bytes 786436
Sparse Core Ops, SparseCore 0:
  635.4 59.0 all-reduce.2
where the time goes:
time: 724 us; the launch traced here: 716 us
  waiting for transfers between devices  392 us (54%)
  local copies, waits for them, and re-layouts  139 us (19%)
  matrix products  82.4 us (11%)
  blocking collectives  45.4 us (6%)
  starting transfers between devices  24.5 us (3%)
  other arithmetic  18.6 us (3%)
  between operations  14.2 us (2%)
    all_to_all x1, waiting for transfers between devices, on_device(): lax.all_to_all(z_im, 'col', split_axis=3, concat_axis=2, tiled=True)  103 us
    all_to_all x1, waiting for transfers between devices, on_device(): lax.all_to_all(z_re, 'col', split_axis=3, concat_axis=2, tiled=True)  88 us
    all_to_all x1, waiting for transfers between devices, on_device(): lax.all_to_all(y_re, 'row', split_axis=2, concat_axis=1, tiled=True)  75.7 us
    all_to_all x1, waiting for transfers between devices, on_device(): lax.all_to_all(y_im, 'row', split_axis=2, concat_axis=1, tiled=True)  66.2 us
    psum x1, waiting for transfers between devices, spread(): return lax.psum(block, axis)  59.1 us
    all_gather x1, blocking collectives, on_device(): lax.all_gather(m_im, 'col', axis=1, tiled=True)  23.4 us
    all_gather x1, blocking collectives, on_device(): lax.all_gather(m_re, 'col', axis=1, tiled=True)  22 us
    all_to_all x2, local copies, waits for them, and re-layouts, on_device(): lax.all_to_all(z_re, 'col', split_axis=3, concat_axis=2, tiled=True)  20.7 us
  transfers between devices with their start and end apart: 5, of which 5 were waited for; matrix products, arithmetic and copies ran while one was open for 14% of the time, Pallas kernels for 0%

commit v1 on v0

v1 whole, which is shorter than its diff:
```python
import math

import jax
import jax.numpy as jnp
from jax import lax
from jax.sharding import PartitionSpec as P

GRID = 128
NG = 8192


HIGH = lax.Precision.HIGHEST


def phase_table(left, right, length):
    phase = left[:, None] * right[None, :] % length
    angle = phase.astype(jnp.float32) * (2.0 * math.pi / length)
    return (jnp.cos(angle), jnp.sin(angle))


def contract_pairs(left, right):
    return lax.dot_general(
        left, right, (((0,), (0,)), ((), ())), precision=HIGH, preferred_element_type=jnp.float32
    )


def on_device(psi_val, psi_cond, eps_val, eps_cond, val_index, cond_index, gmap, chi0_in):
    pairs = val_index.shape[0]
    scale = 1.0 / math.sqrt(GRID**3)
    row_pos = lax.axis_index("row")
    col_pos = lax.axis_index("col")
    mesh_cols = lax.axis_size("col")
    mesh_rows = lax.axis_size("row")
    per_device = NG // (mesh_rows * mesh_cols)
    row_span = GRID // mesh_rows
    col_span = GRID // mesh_cols
    steps = jnp.arange(GRID, dtype=jnp.int32)

    rho = jnp.take(psi_val, val_index, axis=0) * jnp.take(psi_cond, cond_index, axis=0)

    cos_z, sin_z = phase_table(steps, steps, GRID)
    table_z = jnp.stack([cos_z, -sin_z], axis=-1).reshape(GRID, mesh_cols, col_span, 2)
    z_all = jnp.einsum("pxyz,zckt->cpxykt", rho, table_z, precision=HIGH)
    z_mine = lax.all_to_all(z_all, "col", split_axis=0, concat_axis=0, tiled=True)

    cos_y, sin_y = phase_table(steps, steps, GRID)
    table_y = jnp.stack(
        [jnp.stack([cos_y, -sin_y], axis=-1), jnp.stack([sin_y, cos_y], axis=-1)], axis=1
    ).reshape(mesh_cols, col_span, 2, GRID, 2)
    y_all = jnp.einsum("spxykt,syteu->pxeku", z_mine, table_y, precision=HIGH)

    col_map = lax.dynamic_index_in_dim(
        gmap.reshape(mesh_rows, mesh_cols, per_device), col_pos, axis=1, keepdims=False
    ).reshape(-1)
    freq_x = col_map // (GRID * GRID)
    freq_y = col_map // GRID % GRID
    freq_z = col_map % GRID - col_pos * col_span
    pick = freq_y * col_span + freq_z
    flat = y_all.reshape(pairs, row_span, GRID * col_span, 2)
    chosen = jnp.take(flat, pick, axis=2)
    x_glob = row_pos * row_span + jnp.arange(row_span, dtype=jnp.int32)
    cos_x, sin_x = phase_table(x_glob, freq_x, GRID)
    c_re = chosen[..., 0]
    c_im = chosen[..., 1]
    part_re = jnp.sum(c_re * cos_x[None] + c_im * sin_x[None], axis=1)
    part_im = jnp.sum(c_im * cos_x[None] - c_re * sin_x[None], axis=1)
    partial = jnp.stack([part_re, part_im], axis=0) * scale
    own = lax.psum_scatter(partial, "row", scatter_dimension=2, tiled=True)

    rows = lax.all_gather(own, "col", axis=2, tiled=True)
    half = mesh_cols // 2
    send = lax.dynamic_slice_in_dim(rows, (col_pos // half) * half * per_device, half * per_device, 2)
    perm = []
    for src_r in range(mesh_rows):
        for src_c in range(mesh_cols):
            dst_r = src_c % half
            dst_c = 2 * src_r + src_c // half
            perm.append((src_r * mesh_cols + src_c, dst_r * mesh_cols + dst_c))
    cols = lax.ppermute(send, ("row", "col"), perm)

    val_hot = val_index[:, None] == jnp.arange(eps_val.shape[0], dtype=jnp.int32)[None, :]
    cond_hot = cond_index[:, None] == jnp.arange(eps_cond.shape[0], dtype=jnp.int32)[None, :]
    energy_v = jnp.sum(jnp.where(val_hot, eps_val[None, :], 0.0), axis=1)
    energy_c = jnp.sum(jnp.where(cond_hot, eps_cond[None, :], 0.0), axis=1)
    weight = (-6.0 / (math.sqrt(pairs) * (energy_c - energy_v)))[:, None]
    rows_re = rows[0]
    rows_im = rows[1]
    cols_re = cols[0]
    cols_im = cols[1]
    out_re = (
        chi0_in[0]
        + contract_pairs(weight * rows_re, cols_re)
        + contract_pairs(weight * rows_im, cols_im)
    )
    out_im = (
        chi0_in[1]
        + contract_pairs(weight * rows_im, cols_re)
        - contract_pairs(weight * rows_re, cols_im)
    )
    return jnp.stack([out_re, out_im])


def solution(mesh):
    return jax.shard_map(
        on_device,
        mesh=mesh,
        in_specs=(
            P(None, "row", "col", None),
            P(None, "row", "col", None),
            P(),
            P(),
            P(),
            P(),
            P(),
            P(None, "row", "col"),
        ),
        out_specs=P(None, "row", "col"),
        check_vma=False,
    )
```

time: 724 us -> 587 us (0.81)
  local copies, waits for them, and re-layouts: 139 us -> 83.9 us
  blocking collectives: 45.4 us -> 0 us
  matrix products: 82.4 us -> 59 us
  starting transfers between devices: 24.5 us -> 13.3 us
    all_to_all x4 -> x1, waiting for transfers between devices: 333 us -> 243 us  [on_device(): lax.all_to_all(z_all, 'col', split_axis=0, concat_axis=0, tiled=True)]
    unnamed x1 -> x3, waiting for transfers between devices: 0.02 us -> 61.3 us
    psum x1 -> x0, waiting for transfers between devices: 59.1 us -> none  [spread(): return lax.psum(block, axis)]
    all_to_all x6 -> x0, local copies, waits for them, and re-layouts: 57 us -> none  [the longest x2 20.7 us: on_device(): lax.all_to_all(z_re, 'col', split_axis=3, concat_axis=2, tiled=True)]
    all_gather x2 -> x0, blocking collectives: 45.4 us -> none  [the longest x1 23.4 us: on_device(): lax.all_gather(m_im, 'col', axis=1, tiled=True)]
    ppermute x0 -> x1, waiting for transfers between devices: none -> 44 us  [on_device(): cols = lax.ppermute(send, ('row', 'col'), perm)]
    all_gather x0 -> x1, waiting for transfers between devices: none -> 42 us  [on_device(): rows = lax.all_gather(own, 'col', axis=2, tiled=True)]
    transpose x0 -> x2, local copies, waits for them, and re-layouts: none -> 28 us  [the longest x1 17.4 us: on_device(): y_all = jnp.einsum('spxykt,syteu->pxeku', z_mine, table_y, precision=HIGH)]
  transfers between devices with their start and end apart: 5 -> 4, of which waited for: 5 -> 4; matrix products, arithmetic and copies ran while one was open for 14% -> 1% of each run, Pallas kernels for 0% -> 0%
where the time goes in v1:
time: 587 us; the launch traced here: 584 us
  waiting for transfers between devices  390 us (66%)
  local copies, waits for them, and re-layouts  83.9 us (14%)
  matrix products  59 us (10%)
  other arithmetic  23.5 us (4%)
  between operations  14.8 us (3%)
  starting transfers between devices  13.3 us (2%)
    all_to_all x1, waiting for transfers between devices, on_device(): lax.all_to_all(z_all, 'col', split_axis=0, concat_axis=0, tiled=True)  243 us
    unnamed x3, waiting for transfers between devices  61.3 us
    ppermute x1, waiting for transfers between devices, on_device(): cols = lax.ppermute(send, ('row', 'col'), perm)  44 us
    all_gather x1, waiting for transfers between devices, on_device(): rows = lax.all_gather(own, 'col', axis=2, tiled=True)  42 us
    dot_general x1, matrix products, on_device(): y_all = jnp.einsum('spxykt,syteu->pxeku', z_mine, table_y, precision=HIGH)  33.6 us
    reshape x1, local copies, waits for them, and re-layouts, on_device(): flat = y_all.reshape(pairs, row_span, GRID * col_span, 2)  22.9 us
    dot_general x1, matrix products, on_device(): z_all = jnp.einsum('pxyz,zckt->cpxykt', rho, table_z, precision=HIGH)  17.9 us
    transpose x1, local copies, waits for them, and re-layouts, on_device(): y_all = jnp.einsum('spxykt,syteu->pxeku', z_mine, table_y, precision=HIGH)  17.4 us
  transfers between devices with their start and end apart: 4, of which 4 were waited for; matrix products, arithmetic and copies ran while one was open for 1% of the time, Pallas kernels for 0%

profile of v1, /device:TPU:24, one launch (start us, length us, event | category | flops | bytes accessed | tf_op | source)
XLA Modules:
  0.0 584.2 jit_solution(13690530051761402167)
XLA Ops:
  6.5 0.7 compare_select_fusion.7
  7.2 0.7 compare_and_fusion
  7.9 0.1 copy.39
  8.0 0.3 fusion.34
  8.3 6.5 %gather_fusion.2 = f32[128,16,8,128]{3,2,1,0:T(8,128)} fusion(f32[64,16,8,128]{3,2,1,0:T(8,128)} %param.11, s32[1024]{0:T(1024)S(1)} %pad_clamp_fusion.1), kind=kCustom, calls=%fused_computation.1.clone | custom fusion | bytes 16777728 | tf_op jit(solution)/shard_map/jit(_take)/gather | solution.py:39
  14.8 6.5 %gather_fusion.1 = f32[128,16,8,128]{3,2,1,0:T(8,128)} fusion(f32[64,16,8,128]{3,2,1,0:T(8,128)} %param.10, s32[1024]{0:T(1024)S(1)} %pad_clamp_fusion.2), kind=kCustom, calls=%fused_computation.clone | custom fusion | bytes 16777728 | tf_op jit(solution)/shard_map/jit(_take)/gather | solution.py:39
  21.4 6.7 %fusion.4 = f32[128,16,8,128,1,1]{3,2,1,0,5,4:T(8,128)S(1)} fusion(f32[128,16,8,128]{3,2,1,0:T(8,128)} %gather_fusion.2, f32[128,16,8,128]{3,2,1,0:T(8,128)} %gather_fusion.1, pred[128]{0:T(512)(128)(4,1)S(1)} %get-tuple-element.25, pred[128]{0:T(512)(128)(4,1)S(1)} %get-tuple-element.26), kind=kLoop, calls=%fused_computation.10 | loop fusion | flops 6291456 | bytes 25166080 | tf_op jit(solution)/shard_map/mul | solution.py:39
  28.1 17.9 %convolution_bitcast_fusion = f32[16,128,16,8,8,2]{1,0,3,5,4,2:T(8,128)S(1)} fusion(f32[128,16,8,128,1,1]{3,2,1,0,5,4:T(8,128)S(1)} %fusion.4, f32[128,16,8,2,1,1]{0,2,3,1,5,4:T(8,128)S(1)} %maximum_bitcast_fusion.2), kind=kOutput, calls=%fused_computation.7 | convolution fusion | flops 6442450944 | bytes 25296896 | tf_op jit(solution)/shard_map/pxyz,zckt->cpxykt/dot_general | solution.py:43
  46.0 10.6 %copy.42 = f32[16,128,16,8,8,2]{1,3,5,4,2,0:T(8,128)} copy(f32[16,128,16,8,8,2]{1,0,3,5,4,2:T(8,128)S(1)} %convolution_bitcast_fusion) | data formatting | bytes 33554432 | tf_op jit(solution)/shard_map/pxyz,zckt->cpxykt/transpose | solution.py:43
  56.6 7.3 %all-to-all-start = ((f32[16,128,16,8,8,2]{1,3,5,4,2,0:T(8,128)}), f32[16,128,16,8,8,2]{1,3,5,4,2,0:T(8,128)}, u32[]{:S(2)}, u32[]{:S(2)}) async-start(f32[16,128,16,8,8,2]{1,3,5,4,2,0:T(8,128)} %copy.42), calls=%async_computation | async-start | bytes 33554432 | tf_op jit(solution)/shard_map/all_to_all | solution.py:44
  63.9 0.0 all-reduce.3.cloned.1.call-start
  64.0 0.1 reshape.480
  64.0 0.5 broadcast.642
  64.6 0.7 fusion.50
  65.2 0.1 reshape.483
  65.3 0.1 reshape.481
  65.4 0.2 fusion.39
  65.6 0.8 copy.48
  66.5 0.8 copy.46
  67.3 0.5 compare_and_fusion.2
  67.9 0.3 fusion.37
  68.2 242.5 %all-to-all-done = f32[16,128,16,8,8,2]{1,3,5,4,2,0:T(8,128)} async-done(((f32[16,128,16,8,8,2]{1,3,5,4,2,0:T(8,128)}), f32[16,128,16,8,8,2]{1,3,5,4,2,0:T(8,128)}, u32[]{:S(2)}, u32[]{:S(2)}) %all-to-all-start) | async-done | bytes 16777248 | tf_op jit(solution)/shard_map/all_to_all | solution.py:44
  310.8 33.6 %fusion.5 = f32[128,16,128,8,2]{0,2,3,1,4:T(8,128)} fusion(f32[16,128,16,8,8,2]{1,3,5,4,2,0:T(8,128)} %all-to-all-done, f32[16,8,1,128,1]{3,0,1,2,4:T(8,128)S(1)} %get-tuple-element.20, f32[16,8,1,128,1]{3,0,1,2,4:T(8,128)S(1)} %get-tuple-element.19, f32[16,8,1,128,1]{3,0,1,2,4:T(8,128)S(1)} %get-tuple-element.18), kind=kOutput, calls=%fused_computation.12 | convolution fusion | flops 12885098496 | bytes 33751040 | tf_op jit(solution)/shard_map/spxykt,syteu->pxeku/dot_general | solution.py:50
  344.4 17.4 %copy.73 = f32[128,16,128,8,2]{0,3,2,4,1:T(8,128)S(1)} copy(f32[128,16,128,8,2]{0,2,3,1,4:T(8,128)} %fusion.5) | data formatting | bytes 33554432 | tf_op jit(solution)/shard_map/spxykt,syteu->pxeku/transpose | solution.py:50
  361.8 22.9 %copy.45 = f32[128,16,1024,2]{0,1,3,2:T(8,128)} copy(f32[128,16,1024,2]{0,2,3,1:T(8,128)S(1)} %bitcast.74) | data formatting | bytes 33554432 | tf_op jit(solution)/shard_map/reshape | solution.py:59
  384.6 10.1 %gather_fusion = f32[512,128,16,2]{1,2,3,0:T(8,128)} fusion(f32[128,16,1024,2]{0,1,3,2:T(8,128)} %copy.45, s32[1024]{0:T(1024)S(1)} %pad_clamp_fusion), kind=kCustom, calls=%fused_computation.2 | custom fusion | bytes 16779264 | tf_op jit(solution)/shard_map/jit(_take)/gather | solution.py:60
  394.7 4.4 select_bitcast_fusion
  399.1 0.0 copy-start.11
  399.2 6.8 %add_reduce_fusion = (f32[128,512]{0,1:T(8,128)S(1)}, f32[128,512]{0,1:T(8,128)S(1)}) fusion(f32[128,16,512,2]{0,1,3,2:T(8,128)S(1)} %select_bitcast_fusion, f32[16,512]{0,1:T(8,128)S(1)} %copy-done.1, f32[16,512]{0,1:T(8,128)S(1)} %copy-done.2), kind=kLoop, calls=%fused_computation.17 | loop fusion | flops 8257536 | bytes 8978432 | tf_op jit(solution)/shard_map/reduce_sum | solution.py:65
  406.0 1.2 copy.51
  407.2 0.0 all-reduce.3.cloned.1.call-update
  407.2 0.0 all-gather.2.cloned.1.call-start
  407.3 0.6 dynamic-slice
  408.4 61.2 %all-reduce.3.cloned.1.call-done = f32[2,128,512]{1,0,2:T(2,128)} async-done(((f32[2,128,512]{1,0,2:T(2,128)}), f32[2,128,512]{1,0,2:T(2,128)}) %all-reduce.3.cloned.1.call-update) | async-done | bytes 524304
  469.6 1.5 constant_dynamic-slice_fusion
  471.1 0.0 all-gather.2.cloned.1.call-update
  471.1 42.0 %all-gather.2.cloned.1.call-done = f32[2,128,1024]{1,0,2:T(2,128)} async-done(((f32[2,128,64]{1,0,2:T(2,128)}), f32[2,128,1024]{1,0,2:T(2,128)}) %all-gather.2.cloned.1.call-update) | async-done | bytes 1048592 | tf_op jit(solution)/shard_map/all_gather | solution.py:70
  513.2 1.1 constant_dynamic-slice_fusion.1
  514.2 6.0 %collective-permute-start = (f32[2,128,512]{1,0,2:T(2,128)S(1)}, f32[2,128,512]{1,0,2:T(2,128)S(1)}, u32[]{:S(2)}, u32[]{:S(2)}) collective-permute-start(f32[2,128,512]{1,0,2:T(2,128)S(1)} %constant_dynamic-slice_fusion.1), channel_id=1, source_target_pairs={{0,0},{1,16},{2,32},{3,48},{4,64},{5,80},{6,96},{7,112},{8,1},{9,1... | collective-permute-start | bytes 1572872 | tf_op jit(solution)/shard_map/ppermute | solution.py:79
  520.2 0.1 select_reduce_fusion
  520.4 2.6 slice_multiply_fusion
  523.0 44.0 %collective-permute-done = f32[2,128,512]{1,0,2:T(2,128)S(1)} collective-permute-done((f32[2,128,512]{1,0,2:T(2,128)S(1)}, f32[2,128,512]{1,0,2:T(2,128)S(1)}, u32[]{:S(2)}, u32[]{:S(2)}) %collective-permute-start) | collective-permute-done | bytes 524320 | tf_op jit(solution)/shard_map/ppermute | solution.py:79
  567.0 0.4 fusion.51
  567.4 1.8 fusion.52
  569.2 1.8 fusion.54
  571.0 1.8 fusion.53
  572.8 2.1 fusion.11
  575.0 2.0 copy-done.10
  (33 shorter events, 0.2 us)
Async XLA Ops:
  56.6 7.3 %copy-start.3 = (s32[8192]{0:T(1024)S(1)}, s32[8192]{0:T(1024)}, u32[]{:S(2)}) copy-start(s32[8192]{0:T(1024)} %param.16) | copy-start | bytes 98308
  56.6 254.1 %all-to-all-start = ((f32[16,128,16,8,8,2]{1,3,5,4,2,0:T(8,128)}), f32[16,128,16,8,8,2]{1,3,5,4,2,0:T(8,128)}, u32[]{:S(2)}, u32[]{:S(2)}) async-start(f32[16,128,16,8,8,2]{1,3,5,4,2,0:T(8,128)} %copy.42), calls=%async_computation | async-start | bytes 33554432 | tf_op jit(solution)/shard_map/all_to_all | solution.py:44
  63.9 405.7 %all-reduce.3.cloned.1.call-start = ((), (), s32[]{:S(2)}) async-start(), calls=%async_computation.2 | async-start | bytes 1048576
  384.6 10.1 %copy-start.6 = (pred[512]{0:T(512)(128)(4,1)S(1)}, pred[512]{0:T(512)(128)(4,1)}, u32[]{:S(2)}) copy-start(pred[512]{0:T(512)(128)(4,1)} %compare_and_fusion.2) | copy-start | bytes 1540
  394.7 4.4 copy-start.1
  394.7 4.4 copy-start.2
  399.1 8.2 %copy-start.11 = (u32[128]{0:T(128)S(1)}, u32[128]{0:T(128)}, u32[]{:S(2)}) copy-start(u32[128]{0:T(128)} %constant.149) | copy-start | bytes 1540
  399.1 121.1 %copy-start.4 = (s32[128]{0:T(128)S(1)}, s32[128]{0:T(128)}, u32[]{:S(2)}) copy-start(s32[128]{0:T(128)} %param.15) | copy-start | bytes 1540
  399.1 121.1 %copy-start.5 = (s32[128]{0:T(128)S(1)}, s32[128]{0:T(128)}, u32[]{:S(2)}) copy-start(s32[128]{0:T(128)} %param.14) | copy-start | bytes 1540
  399.2 121.1 %copy-start.7 = (f32[64]{0:T(128)S(1)}, f32[64]{0:T(128)}, u32[]{:S(2)}) copy-start(f32[64]{0:T(128)} %param.12) | copy-start | bytes 772
  399.2 121.1 %copy-start.8 = (f32[64]{0:T(128)S(1)}, f32[64]{0:T(128)}, u32[]{:S(2)}) copy-start(f32[64]{0:T(128)} %param.13) | copy-start | bytes 772
  407.2 105.9 %all-gather.2.cloned.1.call-start = ((), (), s32[]{:S(2)}) async-start(), calls=%async_computation.1 | async-start | bytes 1114112 | tf_op jit(solution)/shard_map/all_gather | solution.py:70
  514.2 52.7 %collective-permute-start = (f32[2,128,512]{1,0,2:T(2,128)S(1)}, f32[2,128,512]{1,0,2:T(2,128)S(1)}, u32[]{:S(2)}, u32[]{:S(2)}) collective-permute-start(f32[2,128,512]{1,0,2:T(2,128)S(1)} %constant_dynamic-slice_fusion.1), channel_id=1, source_target_pairs={{0,0},{1,16},{2,32},{3,48},{4,64},{5,80},{6,96},{7,112},{8,1},{9,1... | collective-permute-start | bytes 1572872 | tf_op jit(solution)/shard_map/ppermute | solution.py:79
  520.3 52.4 %copy-start = (f32[2,1024,512]{2,1,0:T(8,128)S(1)}, f32[2,1024,512]{2,1,0:T(8,128)}, u32[]{:S(2)}) copy-start(f32[2,1024,512]{2,1,0:T(8,128)} %param.17) | copy-start | bytes 12582916
  520.4 52.4 %copy-start.9 = (f32[2,1024,512]{2,1,0:T(8,128)S(1)}, f32[2,1024,512]{2,1,0:T(8,128)}, u32[]{:S(2)}) copy-start(f32[2,1024,512]{2,1,0:T(8,128)} %custom-call.6) | copy-start | bytes 12582916
  574.9 2.0 copy-start.10
Sparse Core Ops, SparseCore 0:
  407.3 62.2 all-reduce.2
  472.0 41.1 all-gather.1

commit v2 on v1

--- a/solution.py
+++ b/solution.py
@@ -36,19 +36,6 @@
     col_span = GRID // mesh_cols
     steps = jnp.arange(GRID, dtype=jnp.int32)
 
-    rho = jnp.take(psi_val, val_index, axis=0) * jnp.take(psi_cond, cond_index, axis=0)
-
-    cos_z, sin_z = phase_table(steps, steps, GRID)
-    table_z = jnp.stack([cos_z, -sin_z], axis=-1).reshape(GRID, mesh_cols, col_span, 2)
-    z_all = jnp.einsum("pxyz,zckt->cpxykt", rho, table_z, precision=HIGH)
-    z_mine = lax.all_to_all(z_all, "col", split_axis=0, concat_axis=0, tiled=True)
-
-    cos_y, sin_y = phase_table(steps, steps, GRID)
-    table_y = jnp.stack(
-        [jnp.stack([cos_y, -sin_y], axis=-1), jnp.stack([sin_y, cos_y], axis=-1)], axis=1
-    ).reshape(mesh_cols, col_span, 2, GRID, 2)
-    y_all = jnp.einsum("spxykt,syteu->pxeku", z_mine, table_y, precision=HIGH)
-
     col_map = lax.dynamic_index_in_dim(
         gmap.reshape(mesh_rows, mesh_cols, per_device), col_pos, axis=1, keepdims=False
     ).reshape(-1)
@@ -56,18 +43,40 @@
     freq_y = col_map // GRID % GRID
     freq_z = col_map % GRID - col_pos * col_span
     pick = freq_y * col_span + freq_z
-    flat = y_all.reshape(pairs, row_span, GRID * col_span, 2)
-    chosen = jnp.take(flat, pick, axis=2)
     x_glob = row_pos * row_span + jnp.arange(row_span, dtype=jnp.int32)
     cos_x, sin_x = phase_table(x_glob, freq_x, GRID)
-    c_re = chosen[..., 0]
-    c_im = chosen[..., 1]
-    part_re = jnp.sum(c_re * cos_x[None] + c_im * sin_x[None], axis=1)
-    part_im = jnp.sum(c_im * cos_x[None] - c_re * sin_x[None], axis=1)
-    partial = jnp.stack([part_re, part_im], axis=0) * scale
-    own = lax.psum_scatter(partial, "row", scatter_dimension=2, tiled=True)
 
-    rows = lax.all_gather(own, "col", axis=2, tiled=True)
+    cos_z, sin_z = phase_table(steps, steps, GRID)
+    table_z = jnp.stack([cos_z, -sin_z], axis=-1).reshape(GRID, mesh_cols, col_span, 2)
+    cos_y, sin_y = phase_table(steps, steps, GRID)
+    table_y = jnp.stack(
+        [jnp.stack([cos_y, -sin_y], axis=-1), jnp.stack([sin_y, cos_y], axis=-1)], axis=1
+    ).reshape(mesh_cols, col_span, 2, GRID, 2)
+
+    chunks = 4
+    chunk = pairs // chunks
+    pieces = []
+    for i in range(chunks):
+        v_idx = val_index[i * chunk:(i + 1) * chunk]
+        c_idx = cond_index[i * chunk:(i + 1) * chunk]
+        rho = jnp.take(psi_val, v_idx, axis=0) * jnp.take(psi_cond, c_idx, axis=0)
+        z_all = jnp.einsum("pxyz,zckt->cpxykt", rho, table_z, precision=HIGH)
+        z_mine = lax.all_to_all(z_all, "col", split_axis=0, concat_axis=0, tiled=True)
+        y_all = jnp.einsum("spxykt,syteu->pxeku", z_mine, table_y, precision=HIGH)
+        flat = y_all.reshape(chunk, row_span, GRID * col_span, 2)
+        chosen = jnp.take(flat, pick, axis=2)
+        c_re = chosen[..., 0]
+        c_im = chosen[..., 1]
+        part_re = jnp.sum(c_re * cos_x[None] + c_im * sin_x[None], axis=1)
+        part_im = jnp.sum(c_im * cos_x[None] - c_re * sin_x[None], axis=1)
+        pieces.append(jnp.stack([part_re, part_im], axis=0))
+    partial = jnp.concatenate(pieces, axis=1) * scale
+    spread = partial.reshape(2, pairs, mesh_rows, per_device).transpose(2, 0, 1, 3)
+    gathered = lax.all_to_all(spread, "row", split_axis=0, concat_axis=0, tiled=True)
+    own = jnp.sum(gathered, axis=0)
+    copies = jnp.broadcast_to(own[None], (mesh_cols,) + own.shape)
+    row_blocks = lax.all_to_all(copies, "col", split_axis=0, concat_axis=0, tiled=True)
+    rows = row_blocks.transpose(1, 2, 0, 3).reshape(2, pairs, mesh_cols * per_device)
     half = mesh_cols // 2
     send = lax.dynamic_slice_in_dim(rows, (col_pos // half) * half * per_device, half * per_device, 2)
     perm = []

time: 587 us -> 789 us (1.34); the launches traced: 584 us -> 778 us
  waiting for transfers between devices: 390 us -> 92.3 us
  local copies, waits for them, and re-layouts: 83.9 us -> 298 us
  matrix products: 59 us -> 236 us
  other arithmetic: 23.5 us -> 99.9 us
  starting transfers between devices: 13.3 us -> 34.9 us
  blocking collectives: 0 us -> 15.6 us
  between operations: 14.8 us -> 0.68 us
    all_to_all x1 -> x4, waiting for transfers between devices: 243 us -> 31.6 us  [on_device(): lax.all_to_all(z_all, 'col', split_axis=0, concat_axis=0, tiled=True)]
    dot_general x1 -> x4, matrix products: 33.6 us -> 162 us  [on_device(): y_all = jnp.einsum('spxykt,syteu->pxeku', z_mine, table_y, precision=HIGH)]
    unnamed x26 -> x38, local copies, waits for them, and re-layouts: 4.09 us -> 125 us
    unnamed x3 -> x0, waiting for transfers between devices: 61.3 us -> none
    all_to_all x0 -> x4, other arithmetic: none -> 54.9 us  [on_device(): lax.all_to_all(z_all, 'col', split_axis=0, concat_axis=0, tiled=True)]
    dot_general x1 -> x4, matrix products: 17.9 us -> 66.5 us  [on_device(): z_all = jnp.einsum('pxyz,zckt->cpxykt', rho, table_z, precision=HIGH)]
    all_gather x1 -> x0, waiting for transfers between devices: 42 us -> none  [on_device(): rows = lax.all_gather(own, 'col', axis=2, tiled=True)]
    reshape x1 -> x4, local copies, waits for them, and re-layouts: 22.9 us -> 57.5 us  [on_device(): flat = y_all.reshape(chunk, row_span, GRID * col_span, 2)]
  transfers between devices with their start and end apart: 4 -> 6, of which waited for: 4 -> 5; matrix products, arithmetic and copies ran while one was open for 1% -> 56% of each run, Pallas kernels for 0% -> 0%
where the time goes in v2:
time: 789 us; the launch traced here: 778 us
  local copies, waits for them, and re-layouts  298 us (38%)
  matrix products  236 us (30%)
  other arithmetic  99.9 us (13%)
  waiting for transfers between devices  92.3 us (12%)
  starting transfers between devices  34.9 us (4%)
  blocking collectives  15.6 us (2%)
    dot_general x4, matrix products, on_device(): y_all = jnp.einsum('spxykt,syteu->pxeku', z_mine, table_y, precision=HIGH)  162 us
    unnamed x38, local copies, waits for them, and re-layouts  125 us
    dot_general x4, matrix products, on_device(): z_all = jnp.einsum('pxyz,zckt->cpxykt', rho, table_z, precision=HIGH)  66.5 us
    reshape x4, local copies, waits for them, and re-layouts, on_device(): flat = y_all.reshape(chunk, row_span, GRID * col_span, 2)  57.5 us
    all_to_all x4, other arithmetic, on_device(): lax.all_to_all(z_all, 'col', split_axis=0, concat_axis=0, tiled=True)  54.9 us
    ppermute x1, waiting for transfers between devices, on_device(): cols = lax.ppermute(send, ('row', 'col'), perm)  46.2 us
    transpose x4, local copies, waits for them, and re-layouts, on_device(): z_all = jnp.einsum('pxyz,zckt->cpxykt', rho, table_z, precision=HIGH)  42.7 us
    gather x4, local copies, waits for them, and re-layouts, on_device(): chosen = jnp.take(flat, pick, axis=2)  40.5 us
  transfers between devices with their start and end apart: 6, of which 5 were waited for; matrix products, arithmetic and copies ran while one was open for 56% of the time, Pallas kernels for 0%

profile of v2, /device:TPU:24, one launch (start us, length us, event | category | flops | bytes accessed | tf_op | source)
XLA Modules:
  0.0 777.5 jit_solution(249942802709405474)
XLA Ops:
  10.3 25.7 %convolution_bitcast_fusion.2 = f32[16,32,16,8,8,2]{1,0,3,5,4,2:T(8,128)S(1)} fusion(f32[32,16,8,128,1,1]{3,2,1,0,5,4:T(8,128)S(1)} %fusion.37, f32[128,16,8,2,1,1]{0,2,3,1,5,4:T(8,128)S(1)} %maximum_bitcast_fusion.5), kind=kOutput, calls=%fused_computation.26 | convolution fusion | flops 1610612736 | bytes 6422528 | tf_op jit(solution)/shard_map/pxyz,zckt->cpxykt/dot_general | solution.py:63
  36.1 10.6 %copy.241 = f32[16,32,16,8,8,2]{1,3,5,4,2,0:T(8,128)} copy(f32[16,32,16,8,8,2]{1,0,3,5,4,2:T(8,128)S(1)} %convolution_bitcast_fusion.2) | data formatting | bytes 8388608 | tf_op jit(solution)/shard_map/pxyz,zckt->cpxykt/transpose | solution.py:63
  46.7 16.0 %reshape.534 = f32[16,1,65536]{2,1,0:T(1,128)} reshape(f32[16,16,8,2,8,32]{5,4,3,2,1,0:T(8,128)} %bitcast.227) | data formatting | bytes 8388608
  62.7 7.2 all-to-all-start.1
  78.9 13.7 %convolution_bitcast_fusion.1 = f32[16,32,16,8,8,2]{1,0,3,5,4,2:T(8,128)S(1)} fusion(f32[32,16,8,128,1,1]{3,2,1,0,5,4:T(8,128)S(1)} %fusion.36, f32[128,16,8,2,1,1]{0,2,3,1,5,4:T(8,128)S(1)} %maximum_bitcast_fusion.5), kind=kOutput, calls=%fused_computation.25 | convolution fusion | flops 1610612736 | bytes 6422528 | tf_op jit(solution)/shard_map/pxyz,zckt->cpxykt/dot_general | solution.py:63
  92.5 10.7 %copy.240 = f32[16,32,16,8,8,2]{1,3,5,4,2,0:T(8,128)} copy(f32[16,32,16,8,8,2]{1,0,3,5,4,2:T(8,128)S(1)} %convolution_bitcast_fusion.1) | data formatting | bytes 8388608 | tf_op jit(solution)/shard_map/pxyz,zckt->cpxykt/transpose | solution.py:63
  103.2 16.0 %reshape.536 = f32[16,1,65536]{2,1,0:T(1,128)} reshape(f32[16,16,8,2,8,32]{5,4,3,2,1,0:T(8,128)} %bitcast.228) | data formatting | bytes 8388608
  119.2 12.7 %all-to-all-done.1 = f32[16,1,65536]{2,1,0:T(1,128)} async-done(((f32[16,1,65536]{2,1,0:T(1,128)}), f32[16,1,65536]{2,1,0:T(1,128)}, u32[]{:S(2)}, u32[]{:S(2)}) %all-to-all-start.1) | async-done | bytes 4194336 | tf_op jit(solution)/shard_map/all_to_all | solution.py:64
  131.9 5.9 all-to-all-start.2
  140.6 4.2 gather_fusion.10
  146.8 13.4 %convolution_bitcast_fusion = f32[16,32,16,8,8,2]{1,0,3,5,4,2:T(8,128)S(1)} fusion(f32[32,16,8,128,1,1]{3,2,1,0,5,4:T(8,128)S(1)} %fusion.35, f32[128,16,8,2,1,1]{0,2,3,1,5,4:T(8,128)S(1)} %maximum_bitcast_fusion.5), kind=kOutput, calls=%fused_computation.24 | convolution fusion | flops 1610612736 | bytes 6422528 | tf_op jit(solution)/shard_map/pxyz,zckt->cpxykt/dot_general | solution.py:63
  160.2 10.7 %copy.239 = f32[16,32,16,8,8,2]{1,3,5,4,2,0:T(8,128)} copy(f32[16,32,16,8,8,2]{1,0,3,5,4,2:T(8,128)S(1)} %convolution_bitcast_fusion) | data formatting | bytes 8388608 | tf_op jit(solution)/shard_map/pxyz,zckt->cpxykt/transpose | solution.py:63
  170.9 16.0 %reshape.538 = f32[16,1,65536]{2,1,0:T(1,128)} reshape(f32[16,16,8,2,8,32]{5,4,3,2,1,0:T(8,128)} %bitcast.229) | data formatting | bytes 8388608
  186.9 10.7 %all-to-all-done.2 = f32[16,1,65536]{2,1,0:T(1,128)} async-done(((f32[16,1,65536]{2,1,0:T(1,128)}), f32[16,1,65536]{2,1,0:T(1,128)}, u32[]{:S(2)}, u32[]{:S(2)}) %all-to-all-start.2) | async-done | bytes 4194336 | tf_op jit(solution)/shard_map/all_to_all | solution.py:64
  197.6 5.0 all-to-all-start.3
  211.7 13.7 %convolution_bitcast_fusion.3 = f32[16,32,16,8,8,2]{1,0,3,5,4,2:T(8,128)S(1)} fusion(f32[32,16,8,128,1,1]{3,2,1,0,5,4:T(8,128)S(1)} %fusion.38, f32[128,16,8,2,1,1]{0,2,3,1,5,4:T(8,128)S(1)} %maximum_bitcast_fusion.5), kind=kOutput, calls=%fused_computation.27 | convolution fusion | flops 1610612736 | bytes 6422528 | tf_op jit(solution)/shard_map/pxyz,zckt->cpxykt/dot_general | solution.py:63
  225.3 10.7 %copy.242 = f32[16,32,16,8,8,2]{1,3,5,4,2,0:T(8,128)} copy(f32[16,32,16,8,8,2]{1,0,3,5,4,2:T(8,128)S(1)} %convolution_bitcast_fusion.3) | data formatting | bytes 8388608 | tf_op jit(solution)/shard_map/pxyz,zckt->cpxykt/transpose | solution.py:63
  236.0 16.0 %reshape.532 = f32[16,1,65536]{2,1,0:T(1,128)} reshape(f32[16,16,8,2,8,32]{5,4,3,2,1,0:T(8,128)} %bitcast.230) | data formatting | bytes 8388608
  252.0 8.2 %all-to-all-done.3 = f32[16,1,65536]{2,1,0:T(1,128)} async-done(((f32[16,1,65536]{2,1,0:T(1,128)}), f32[16,1,65536]{2,1,0:T(1,128)}, u32[]{:S(2)}, u32[]{:S(2)}) %all-to-all-start.3) | async-done | bytes 4194336 | tf_op jit(solution)/shard_map/all_to_all | solution.py:64
  260.2 4.7 all-to-all-start
  268.6 13.8 %reduce.7 = f32[16,65536]{1,0:T(8,128)} reduce(f32[16,1,65536]{2,1,0:T(1,128)} %all-to-all-done.1, f32[]{:T(128)} %broadcast.529), dimensions={1}, to_apply=%all_to_all.19.reduce_sub_computation | reduce | bytes 8388612 | tf_op jit(solution)/shard_map/all_to_all | solution.py:64
  282.4 15.3 %reshape.535 = f32[16,16,8,2,8,32]{5,4,3,2,1,0:T(8,128)} reshape(f32[16,65536]{1,0:T(8,128)} %reduce.7) | data formatting | bytes 8388608
  297.7 40.5 %fusion.18 = f32[32,16,128,8,2]{2,0,3,1,4:T(8,128)} fusion(f32[16,32,16,8,8,2]{1,3,5,4,2,0:T(8,128)} %bitcast.224, f32[16,8,1,128,1]{3,0,1,2,4:T(8,128)S(1)} %get-tuple-element.47, f32[16,8,1,128,1]{3,0,1,2,4:T(8,128)S(1)} %get-tuple-element.46, f32[16,8,1,128,1]{3,0,1,2,4:T(8,128)S(1)} %get-tuple-element.45), kind=kOutput, calls=%fused_computation.53 | convolution fusion | flops 3221422080 | bytes 8585216 | tf_op jit(solution)/shard_map/spxykt,syteu->pxeku/dot_general | solution.py:65
  338.1 14.4 %copy.172 = f32[32,16,128,8,2]{0,1,4,3,2:T(8,128)} copy(f32[32,16,128,8,2]{2,0,3,1,4:T(8,128)} %fusion.18) | data formatting | bytes 8388608 | tf_op jit(solution)/shard_map/reshape | solution.py:66
  352.5 13.7 %reduce.6 = f32[16,65536]{1,0:T(8,128)} reduce(f32[16,1,65536]{2,1,0:T(1,128)} %all-to-all-done.2, f32[]{:T(128)} %broadcast.529), dimensions={1}, to_apply=%all_to_all.20.reduce_sub_computation | reduce | bytes 8388612 | tf_op jit(solution)/shard_map/all_to_all | solution.py:64
  366.2 15.3 %reshape.537 = f32[16,16,8,2,8,32]{5,4,3,2,1,0:T(8,128)} reshape(f32[16,65536]{1,0:T(8,128)} %reduce.6) | data formatting | bytes 8388608
  381.5 40.5 %fusion.21 = f32[32,16,128,8,2]{2,0,3,1,4:T(8,128)} fusion(f32[16,32,16,8,8,2]{1,3,5,4,2,0:T(8,128)} %bitcast.225, f32[16,8,1,128,1]{3,0,1,2,4:T(8,128)S(1)} %get-tuple-element.47, f32[16,8,1,128,1]{3,0,1,2,4:T(8,128)S(1)} %get-tuple-element.46, f32[16,8,1,128,1]{3,0,1,2,4:T(8,128)S(1)} %get-tuple-element.45), kind=kOutput, calls=%fused_computation.54 | convolution fusion | flops 3221422080 | bytes 8585216 | tf_op jit(solution)/shard_map/spxykt,syteu->pxeku/dot_general | solution.py:65
  422.0 14.4 %copy.177 = f32[32,16,128,8,2]{0,1,4,3,2:T(8,128)} copy(f32[32,16,128,8,2]{2,0,3,1,4:T(8,128)} %fusion.21) | data formatting | bytes 8388608 | tf_op jit(solution)/shard_map/reshape | solution.py:66
  436.4 10.1 %gather_fusion.5 = f32[512,32,16,2]{1,2,3,0:T(8,128)} fusion(f32[32,16,1024,2]{0,1,3,2:T(8,128)} %bitcast.219, s32[1024]{0:T(1024)S(1)} %pad_clamp_fusion.6), kind=kCustom, calls=%fused_computation.9.clone | custom fusion | bytes 4196352 | tf_op jit(solution)/shard_map/jit(_take)/gather | solution.py:67
  446.5 10.2 %gather_fusion.8 = f32[512,32,16,2]{1,2,3,0:T(8,128)} fusion(f32[32,16,1024,2]{0,1,3,2:T(8,128)} %bitcast.220, s32[1024]{0:T(1024)S(1)} %pad_clamp_fusion.6), kind=kCustom, calls=%fused_computation.10.clone | custom fusion | bytes 4196352 | tf_op jit(solution)/shard_map/jit(_take)/gather | solution.py:67
  456.7 13.7 %reduce.5 = f32[16,65536]{1,0:T(8,128)} reduce(f32[16,1,65536]{2,1,0:T(1,128)} %all-to-all-done.3, f32[]{:T(128)} %broadcast.529), dimensions={1}, to_apply=%all_to_all.21.reduce_sub_computation | reduce | bytes 8388612 | tf_op jit(solution)/shard_map/all_to_all | solution.py:64
  470.4 15.3 %reshape.539 = f32[16,16,8,2,8,32]{5,4,3,2,1,0:T(8,128)} reshape(f32[16,65536]{1,0:T(8,128)} %reduce.5) | data formatting | bytes 8388608
  485.8 40.5 %fusion.24 = f32[32,16,128,8,2]{2,0,3,1,4:T(8,128)} fusion(f32[16,32,16,8,8,2]{1,3,5,4,2,0:T(8,128)} %bitcast.226, f32[16,8,1,128,1]{3,0,1,2,4:T(8,128)S(1)} %copy-done.6, f32[16,8,1,128,1]{3,0,1,2,4:T(8,128)S(1)} %copy-done.4, f32[16,8,1,128,1]{3,0,1,2,4:T(8,128)S(1)} %copy-done.2), kind=kOutput, calls=%fused_computation.55 | convolution fusion | flops 3221422080 | bytes 8585216 | tf_op jit(solution)/shard_map/spxykt,syteu->pxeku/dot_general | solution.py:65
  526.3 14.4 %copy.182 = f32[32,16,128,8,2]{0,1,4,3,2:T(8,128)} copy(f32[32,16,128,8,2]{2,0,3,1,4:T(8,128)} %fusion.24) | data formatting | bytes 8388608 | tf_op jit(solution)/shard_map/reshape | solution.py:66
  540.7 10.1 %gather_fusion.11 = f32[512,32,16,2]{1,2,3,0:T(8,128)} fusion(f32[32,16,1024,2]{0,1,3,2:T(8,128)} %bitcast.222, s32[1024]{0:T(1024)S(1)} %pad_clamp_fusion.6), kind=kCustom, calls=%fused_computation.11.clone | custom fusion | bytes 4196352 | tf_op jit(solution)/shard_map/jit(_take)/gather | solution.py:67
  550.8 13.7 %reduce.4 = f32[16,65536]{1,0:T(8,128)} reduce(f32[16,1,65536]{2,1,0:T(1,128)} %all-to-all-done, f32[]{:T(128)} %broadcast.529), dimensions={1}, to_apply=%all_to_all.18.reduce_sub_computation | reduce | bytes 8388612 | tf_op jit(solution)/shard_map/all_to_all | solution.py:64
  564.5 15.3 %reshape.533 = f32[16,16,8,2,8,32]{5,4,3,2,1,0:T(8,128)} reshape(f32[16,65536]{1,0:T(8,128)} %reduce.4) | data formatting | bytes 8388608
  579.8 40.5 %fusion.15 = f32[32,16,128,8,2]{2,0,3,1,4:T(8,128)} fusion(f32[16,32,16,8,8,2]{1,3,5,4,2,0:T(8,128)} %bitcast.223, f32[16,8,1,128,1]{3,0,1,2,4:T(8,128)S(1)} %copy-done.6, f32[16,8,1,128,1]{3,0,1,2,4:T(8,128)S(1)} %copy-done.4, f32[16,8,1,128,1]{3,0,1,2,4:T(8,128)S(1)} %copy-done.2), kind=kOutput, calls=%fused_computation.52 | convolution fusion | flops 3221422080 | bytes 8585216 | tf_op jit(solution)/shard_map/spxykt,syteu->pxeku/dot_general | solution.py:65
  620.4 14.4 %copy.165 = f32[32,16,128,8,2]{0,1,4,3,2:T(8,128)} copy(f32[32,16,128,8,2]{2,0,3,1,4:T(8,128)} %fusion.15) | data formatting | bytes 8388608 | tf_op jit(solution)/shard_map/reshape | solution.py:66
  634.7 10.1 %gather_fusion.2 = f32[512,32,16,2]{1,2,3,0:T(8,128)} fusion(f32[32,16,1024,2]{0,1,3,2:T(8,128)} %bitcast.221, s32[1024]{0:T(1024)S(1)} %pad_clamp_fusion.6), kind=kCustom, calls=%fused_computation.1.clone | custom fusion | bytes 4196352 | tf_op jit(solution)/shard_map/jit(_take)/gather | solution.py:67
  644.9 4.3 select_bitcast_fusion
  649.2 15.9 %fusion.12 = (f32[32,16,512,2]{0,1,2,3:T(8,128)S(1)}, f32[32,16,512,2]{0,1,2,3:T(8,128)}, f32[32,16,512,2]{0,1,2,3:T(8,128)}) fusion(f32[512,32,16,2]{1,2,3,0:T(8,128)} %gather_fusion.11, pred[512]{0:T(512)(128)(4,1)S(1)} %copy-done.12, f32[512,32,16,2]{1,2,3,0:T(8,128)} %gather_fusion.8, f32[512,32,16,2]{1,2,3,0:T(8,128)} %gather_fusion.5), kind=kLoop, calls=%fused_computation.29 | loop fusion | flops 1572864 | bytes 12583424 | tf_op jit(solution)/shard_map/jit(_take)/select_n | solution.py:67
  665.2 11.5 %add_reduce_fusion.3 = (f32[32,512]{0,1:T(8,128)S(1)}, f32[32,512]{0,1:T(8,128)S(1)}, f32[32,512]{0,1:T(8,128)S(1)}, f32[32,512]{0,1:T(8,128)S(1)}, f32[32,512]{...) fusion(f32[32,16,512,2]{0,1,3,2:T(8,128)S(1)} %select_bitcast_fusion, ...), kind=kLoop, calls=%fused_computation.51 | loop fusion | flops 8257536 | bytes 8978432 | tf_op jit(solution)/shard_map/reduce_sum | solution.py:70
  677.2 15.6 %all_to_all.30 = f32[8,2,128,64]{2,3,1,0:T(8,128)S(1)} all-to-all(f32[8,2,128,64]{2,3,1,0:T(8,128)S(1)} %fusion.39), channel_id=1, replica_groups=mesh['row'=8,'col'=16] {'row'}, dimensions={0} | all-to-all | bytes 1048576 | tf_op jit(solution)/shard_map/all_to_all | solution.py:75
  693.9 7.2 all-to-all-start.5
  701.1 14.5 %all-to-all-done.5 = f32[16,2,128,64]{2,3,1,0:T(8,128)S(1)} async-done(((f32[16,2,128,64]{2,3,1,0:T(8,128)}), f32[16,2,128,64]{2,3,1,0:T(8,128)S(1)}, u32[]{:S(2)}, u32[]{:S(2)}) %all-to-all-start.5) | async-done | bytes 1048608 | tf_op jit(solution)/shard_map/all_to_all | solution.py:78
  715.8 5.0 collective-permute-start
  721.0 46.2 %collective-permute-done = f32[2,128,512]{1,2,0:T(8,128)S(1)} collective-permute-done((f32[2,128,512]{1,2,0:T(8,128)S(1)}, f32[2,128,512]{1,2,0:T(8,128)S(1)}, u32[]{:S(2)}, u32[]{:S(2)}) %collective-permute-start) | collective-permute-done | bytes 524320 | tf_op jit(solution)/shard_map/ppermute | solution.py:88
  (80 shorter events, 48.8 us)
Async XLA Ops:
  62.7 69.2 %all-to-all-start.1 = ((f32[16,1,65536]{2,1,0:T(1,128)}), f32[16,1,65536]{2,1,0:T(1,128)}, u32[]{:S(2)}, u32[]{:S(2)}) async-start(f32[16,1,65536]{2,1,0:T(1,128)} %reshape.534), calls=%async_computation.1 | async-start | bytes 8388608 | tf_op jit(solution)/shard_map/all_to_all | solution.py:64
  131.9 65.7 %all-to-all-start.2 = ((f32[16,1,65536]{2,1,0:T(1,128)}), f32[16,1,65536]{2,1,0:T(1,128)}, u32[]{:S(2)}, u32[]{:S(2)}) async-start(f32[16,1,65536]{2,1,0:T(1,128)} %reshape.536), calls=%async_computation.2 | async-start | bytes 8388608 | tf_op jit(solution)/shard_map/all_to_all | solution.py:64
  197.6 62.6 %all-to-all-start.3 = ((f32[16,1,65536]{2,1,0:T(1,128)}), f32[16,1,65536]{2,1,0:T(1,128)}, u32[]{:S(2)}, u32[]{:S(2)}) async-start(f32[16,1,65536]{2,1,0:T(1,128)} %reshape.538), calls=%async_computation.3 | async-start | bytes 8388608 | tf_op jit(solution)/shard_map/all_to_all | solution.py:64
  252.0 12.9 %copy-start.9 = (s32[8192]{0:T(1024)S(1)}, s32[8192]{0:T(1024)}, u32[]{:S(2)}) copy-start(s32[8192]{0:T(1024)} %param.18) | copy-start | bytes 98308
  260.2 290.6 %all-to-all-start = ((f32[16,1,65536]{2,1,0:T(1,128)}), f32[16,1,65536]{2,1,0:T(1,128)}, u32[]{:S(2)}, u32[]{:S(2)}) async-start(f32[16,1,65536]{2,1,0:T(1,128)} %reshape.532), calls=%async_computation | async-start | bytes 8388608 | tf_op jit(solution)/shard_map/all_to_all | solution.py:64
  267.9 113.6 %copy-start.1 = (f32[16,8,1,128,1]{3,0,1,2,4:T(8,128)}, f32[16,8,1,128,1]{3,0,1,2,4:T(8,128)S(1)}, u32[]{:S(2)}) copy-start(f32[16,8,1,128,1]{3,0,1,2,4:T(8,128)S(1)} %get-tuple-element.45) | copy-start | bytes 196612
  267.9 113.6 %copy-start.3 = (f32[16,8,1,128,1]{3,0,1,2,4:T(8,128)}, f32[16,8,1,128,1]{3,0,1,2,4:T(8,128)S(1)}, u32[]{:S(2)}) copy-start(f32[16,8,1,128,1]{3,0,1,2,4:T(8,128)S(1)} %get-tuple-element.46) | copy-start | bytes 196612
  268.0 113.6 %copy-start.5 = (f32[16,8,1,128,1]{3,0,1,2,4:T(8,128)}, f32[16,8,1,128,1]{3,0,1,2,4:T(8,128)S(1)}, u32[]{:S(2)}) copy-start(f32[16,8,1,128,1]{3,0,1,2,4:T(8,128)S(1)} %get-tuple-element.47) | copy-start | bytes 196612
  470.4 15.3 %copy-start.2 = (f32[16,8,1,128,1]{3,0,1,2,4:T(8,128)S(1)}, f32[16,8,1,128,1]{3,0,1,2,4:T(8,128)}, u32[]{:S(2)}) copy-start(f32[16,8,1,128,1]{3,0,1,2,4:T(8,128)} %copy-done.1) | copy-start | bytes 196612
  470.4 15.3 %copy-start.4 = (f32[16,8,1,128,1]{3,0,1,2,4:T(8,128)S(1)}, f32[16,8,1,128,1]{3,0,1,2,4:T(8,128)}, u32[]{:S(2)}) copy-start(f32[16,8,1,128,1]{3,0,1,2,4:T(8,128)} %copy-done.3) | copy-start | bytes 196612
  470.4 15.4 %copy-start.6 = (f32[16,8,1,128,1]{3,0,1,2,4:T(8,128)S(1)}, f32[16,8,1,128,1]{3,0,1,2,4:T(8,128)}, u32[]{:S(2)}) copy-start(f32[16,8,1,128,1]{3,0,1,2,4:T(8,128)} %copy-done.5) | copy-start | bytes 196612
  634.7 10.1 %copy-start.12 = (pred[512]{0:T(512)(128)(4,1)S(1)}, pred[512]{0:T(512)(128)(4,1)}, u32[]{:S(2)}) copy-start(pred[512]{0:T(512)(128)(4,1)} %get-tuple-element.33) | copy-start | bytes 1540
  649.2 16.0 %copy-start.7 = (f32[16,512]{0,1:T(8,128)S(1)}, f32[16,512]{0,1:T(8,128)}, u32[]{:S(2)}) copy-start(f32[16,512]{0,1:T(8,128)} %copy.113) | copy-start | bytes 98308
  649.2 15.9 %copy-start.8 = (f32[16,512]{0,1:T(8,128)S(1)}, f32[16,512]{0,1:T(8,128)}, u32[]{:S(2)}) copy-start(f32[16,512]{0,1:T(8,128)} %copy.115) | copy-start | bytes 98308
  677.1 43.6 %copy-start.10 = (s32[128]{0:T(128)S(1)}, s32[128]{0:T(128)}, u32[]{:S(2)}) copy-start(s32[128]{0:T(128)} %param.17) | copy-start | bytes 1540
  677.1 43.6 %copy-start.11 = (s32[128]{0:T(128)S(1)}, s32[128]{0:T(128)}, u32[]{:S(2)}) copy-start(s32[128]{0:T(128)} %param.16) | copy-start | bytes 1540
  677.2 43.6 %copy-start.13 = (f32[64]{0:T(128)S(1)}, f32[64]{0:T(128)}, u32[]{:S(2)}) copy-start(f32[64]{0:T(128)} %param.14) | copy-start | bytes 772
  677.2 43.6 %copy-start.14 = (f32[64]{0:T(128)S(1)}, f32[64]{0:T(128)}, u32[]{:S(2)}) copy-start(f32[64]{0:T(128)} %param.15) | copy-start | bytes 772
  693.9 21.7 %all-to-all-start.5 = ((f32[16,2,128,64]{2,3,1,0:T(8,128)}), f32[16,2,128,64]{2,3,1,0:T(8,128)S(1)}, u32[]{:S(2)}, u32[]{:S(2)}) async-start(f32[16,2,128,64]{2,3,1,0:T(8,128)} %broadcast_in_dim.37), calls=%async_computation.5 | async-start | bytes 2097152 | tf_op jit(solution)/shard_map/all_to_all | solution.py:78
  715.8 55.1 %copy-start = (f32[2,1024,512]{2,1,0:T(8,128)S(1)}, f32[2,1024,512]{2,1,0:T(8,128)}, u32[]{:S(2)}) copy-start(f32[2,1024,512]{2,1,0:T(8,128)} %param.19) | copy-start | bytes 12582916
  715.8 51.4 %collective-permute-start = (f32[2,128,512]{1,2,0:T(8,128)S(1)}, f32[2,128,512]{1,2,0:T(8,128)S(1)}, u32[]{:S(2)}, u32[]{:S(2)}) collective-permute-start(f32[2,128,512]{1,2,0:T(8,128)S(1)} %constant_dynamic-slice_fusion), channel_id=1, source_target_pairs={{0,0},{1,16},{2,32},{3,48},{4,64},{5,80},{6,96},{7,112},{8,1},{9,1... | collective-permute-start | bytes 1572872 | tf_op jit(solution)/shard_map/ppermute | solution.py:88
